TPU v7x, 32 devices: a whole 2x2x4 slice. The times are simulated.
32 devices in a mesh: groups: 2 (over y), dom: 4 (over x, core), sub: 4 (over z).
Axes of the slice: x: 2, y: 2, z: 4, core: 2. Of those that a mesh axis runs over, the one named last changes fastest.
Arguments:
- node_states: float32 [8192, 512], P(('groups', 'dom', 'sub')), parts along dimension 0, may hold values from -6 to 6
- node_pre: float32 [8192, 512], P(('groups', 'dom', 'sub')), parts along dimension 0, may hold values from -6 to 6
- edge_states: float32 [4096, 512], P(('groups', 'dom', 'sub')), parts along dimension 0, may hold values from -6 to 6
- edge_pre: float32 [4096, 512], P(('groups', 'dom', 'sub')), parts along dimension 0, may hold values from -6 to 6
- node_cotangent: float32 [8192, 512], P(('groups', 'dom', 'sub')), parts along dimension 0, may hold values from -6 to 6
- edge_cotangent: float32 [4096, 512], P(('groups', 'dom', 'sub')), parts along dimension 0, may hold values from -6 to 6
- endpoints: int32 [2, 4096], P(None, ('groups', 'dom', 'sub')), parts along dimension 1, may hold values from 0 to 319, as said below
- send_lists: int32 [32, 4, 16], P(('groups', 'dom', 'sub')), parts along dimension 0, may hold values from 0 to 255, as said below
- node_counts: int32 [32], P(('groups', 'dom', 'sub')), parts along dimension 0, may hold values from 128 to 256
- edge_blocks: int32 [32], P(('groups', 'dom', 'sub')), parts along dimension 0, may hold values from 1 to 1
- edge_first: float32 [1536, 512], P(('dom', 'sub')), may hold values from -0.15625 to 0.15625
- edge_second: float32 [512, 512], P(('dom', 'sub')), may hold values from -0.25 to 0.25
- edge_bias: float32 [512], P(('dom', 'sub')), may hold values from -3 to 3
- edge_gain: float32 [512], P(('dom', 'sub')), may hold values from 0.5 to 1.5
- edge_shift: float32 [512], P(('dom', 'sub')), may hold values from -3 to 3
- node_first: float32 [1024, 512], P(('dom', 'sub')), may hold values from -0.1875 to 0.1875
- node_second: float32 [512, 512], P(('dom', 'sub')), may hold values from -0.25 to 0.25
- node_bias: float32 [512], P(('dom', 'sub')), may hold values from -3 to 3
- node_gain: float32 [512], P(('dom', 'sub')), may hold values from 0.5 to 1.5
Outputs:
- edge_grads: float32 [4096, 512], P(('groups', 'dom', 'sub')), parts along dimension 0
- node_grads: float32 [8192, 512], P(('groups', 'dom', 'sub')), parts along dimension 0
- edge_first_grad: float32 [3072, 512], P(('groups', 'dom', 'sub')), parts along dimension 0
- edge_second_grad: float32 [1024, 512], P(('groups', 'dom', 'sub')), parts along dimension 0
- node_first_grad: float32 [2048, 512], P(('groups', 'dom', 'sub')), parts along dimension 0
- node_second_grad: float32 [1024, 512], P(('groups', 'dom', 'sub')), parts along dimension 0
There are 2 independent parts, one for each index of `groups`. A program takes and returns all parts, laid end to end along the dimension named above; an argument that names none is the same for every part. Nothing has to cross between parts.
Inputs may be any that keep to these rules, and one draw needn't show every extreme that they name: `endpoints`: sender slots are a live local node below node_counts of the device, or a ghost slot 256 + k * 16 + j whose neighbour k exists; receiver slots are live local nodes. `send_lists`: every entry is a live node of its device.
All inputs are finite; a program needn't handle non-finite values.
Results may differ from a plain program's by a relative error of at most 0.0003.
Values sent between devices are 32-bit elements; how exact they have to be, the bound alone decides.
No kernel may reach another device: no remote copies, remote signals or barrier semaphores. Data moves between devices by JAX's collectives and lax.ppermute only.
A program may use at most 128 MiB of HBM per device.

v0:
```python
import math
import jax
import jax.numpy as jnp
from jax import lax
from jax.sharding import PartitionSpec as P

EPSILON = 1e-05


def padded(cells, sides, width):
    for axis, dim in sides:
        count = lax.axis_size(axis)
        ends = count - 1
        head = lax.slice_in_dim(cells, 0, width, axis=dim)
        tail = lax.slice_in_dim(cells, cells.shape[dim] - width, cells.shape[dim], axis=dim)
        cells = jnp.concatenate(
            [
                lax.ppermute(tail, axis, [(i, (i + 1) % count) for i in range(ends)]),
                cells,
                lax.ppermute(head, axis, [((i + 1) % count, i) for i in range(ends)]),
            ],
            axis=dim,
        )
    return cells


def matmul(left, right):
    return jnp.dot(left, right, precision=lax.Precision.HIGHEST, preferred_element_type=jnp.float32)


def inner(left, right):
    return lax.dot_general(
        left,
        right,
        (((0,), (0,)), ((), ())),
        precision=lax.Precision.HIGHEST,
        preferred_element_type=jnp.float32,
    )


def outer_back(left, right):
    return lax.dot_general(
        left,
        right,
        (((1,), (1,)), ((), ())),
        precision=lax.Precision.HIGHEST,
        preferred_element_type=jnp.float32,
    )


def layer_norm(values):
    center = values - jnp.mean(values, axis=-1, keepdims=True)
    inverse = 1.0 / jnp.sqrt(jnp.mean(center * center, axis=-1, keepdims=True) + EPSILON)
    return (center * inverse, inverse)


def norm_back(upstream, normed, inverse):
    first = jnp.mean(upstream, axis=-1, keepdims=True)
    second = jnp.mean(upstream * normed, axis=-1, keepdims=True)
    return inverse * (upstream - first - normed * second)


def shards(
    node_states,
    node_pre,
    edge_states,
    edge_pre,
    node_cotangent,
    edge_cotangent,
    endpoints,
    send_lists,
    node_counts,
    edge_blocks,
    edge_first,
    edge_second,
    edge_bias,
    edge_gain,
    edge_shift,
    node_first,
    node_second,
    node_bias,
    node_gain,
):
    node_rows, width = node_states.shape
    edge_rows = edge_states.shape[0]
    ghost = send_lists.shape[2]
    dom_count = lax.axis_size("dom")
    sub_count = lax.axis_size("sub")
    peer_count = dom_count * sub_count
    lists = send_lists[0]
    outgoing = jnp.take(node_states, lists.reshape(-1), axis=0).reshape(4, ghost, width)
    dom_side = padded(jnp.stack([outgoing[1], outgoing[0]]), (("dom", 0),), 1)
    sub_side = padded(jnp.stack([outgoing[3], outgoing[2]]), (("sub", 0),), 1)
    ghosts = jnp.stack([dom_side[0], dom_side[3], sub_side[0], sub_side[3]])
    ghosts = ghosts.reshape(4 * ghost, width)
    full_node_first, full_node_second, full_node_bias, full_node_gain = (
        lax.all_gather(node_first, ("dom", "sub"), axis=0, tiled=True),
        lax.all_gather(node_second, ("dom", "sub"), axis=0, tiled=True),
        lax.all_gather(node_bias, ("dom", "sub"), axis=0, tiled=True),
        lax.all_gather(node_gain, ("dom", "sub"), axis=0, tiled=True),
    )
    full_edge_first, full_edge_second, full_edge_bias, full_edge_gain, full_edge_shift = (
        lax.all_gather(edge_first, ("dom", "sub"), axis=0, tiled=True),
        lax.all_gather(edge_second, ("dom", "sub"), axis=0, tiled=True),
        lax.all_gather(edge_bias, ("dom", "sub"), axis=0, tiled=True),
        lax.all_gather(edge_gain, ("dom", "sub"), axis=0, tiled=True),
        lax.all_gather(edge_shift, ("dom", "sub"), axis=0, tiled=True),
    )
    live_nodes = (jnp.arange(node_rows) < node_counts[0]).astype(jnp.float32)[:, None]
    live_edges = (jnp.arange(edge_rows) < edge_blocks[0] * 128).astype(jnp.float32)[:, None]
    source = endpoints[0]
    target = endpoints[1]
    edge_scale = 1.0 / math.sqrt(edge_rows * peer_count)
    node_scale = 1.0 / math.sqrt(node_rows * peer_count)
    edge_act = jnp.maximum(edge_pre, 0.0)
    edge_normed, edge_inverse = layer_norm(matmul(edge_act, full_edge_second) + full_edge_bias)
    message = (edge_normed * full_edge_gain + full_edge_shift) * live_edges
    aggregate = jax.ops.segment_sum(message, target, node_rows)
    node_act = jnp.maximum(node_pre, 0.0)
    node_normed, node_inverse = layer_norm(matmul(node_act, full_node_second) + full_node_bias)
    node_upstream = node_cotangent * live_nodes
    node_grad_z = norm_back(node_upstream * full_node_gain, node_normed, node_inverse)
    node_grad_pre = outer_back(node_grad_z, full_node_second) * (node_pre > 0).astype(jnp.float32)
    node_input = jnp.concatenate([node_states, aggregate], axis=1)
    node_first_grad, node_second_grad = (
        lax.psum_scatter(
            inner(node_input, node_grad_pre) * node_scale,
            ("dom", "sub"),
            scatter_dimension=0,
            tiled=True,
        ),
        lax.psum_scatter(
            inner(node_act, node_grad_z) * node_scale,
            ("dom", "sub"),
            scatter_dimension=0,
            tiled=True,
        ),
    )
    node_grad_input = outer_back(node_grad_pre, full_node_first)
    state_grads = node_upstream + node_grad_input[:, :width]
    edge_upstream = (
        edge_cotangent + jnp.take(node_grad_input[:, width:], target, axis=0)
    ) * live_edges
    edge_grad_z = norm_back(edge_upstream * full_edge_gain, edge_normed, edge_inverse)
    edge_grad_pre = outer_back(edge_grad_z, full_edge_second) * (edge_pre > 0).astype(jnp.float32)
    edge_second_grad = lax.psum_scatter(
        inner(edge_act, edge_grad_z) * edge_scale, ("dom", "sub"), scatter_dimension=0, tiled=True
    )
    extended = jnp.concatenate([node_states, ghosts], axis=0)
    features = jnp.concatenate(
        [edge_states, jnp.take(extended, source, axis=0), jnp.take(extended, target, axis=0)],
        axis=1,
    )
    edge_first_grad = lax.psum_scatter(
        inner(features, edge_grad_pre) * edge_scale, ("dom", "sub"), scatter_dimension=0, tiled=True
    )
    edge_grad_input = outer_back(edge_grad_pre, full_edge_first)
    edge_grads = (edge_cotangent + edge_grad_input[:, :width]) * live_edges
    extended_grads = jax.ops.segment_sum(
        edge_grad_input[:, width : 2 * width], source, node_rows + 4 * ghost
    )
    extended_grads = extended_grads + jax.ops.segment_sum(
        edge_grad_input[:, 2 * width :], target, node_rows + 4 * ghost
    )
    state_grads = state_grads + extended_grads[:node_rows]
    ghost_grads = extended_grads[node_rows:].reshape(4, ghost, width)
    dom_back = padded(jnp.stack([ghost_grads[0], ghost_grads[1]]), (("dom", 0),), 1)
    sub_back = padded(jnp.stack([ghost_grads[2], ghost_grads[3]]), (("sub", 0),), 1)
    returned = jnp.stack([dom_back[3], dom_back[0], sub_back[3], sub_back[0]])
    state_grads = state_grads + jax.ops.segment_sum(
        returned.reshape(-1, width), lists.reshape(-1), node_rows
    )
    return (
        edge_grads,
        state_grads,
        edge_first_grad,
        edge_second_grad,
        node_first_grad,
        node_second_grad,
    )


def solution(mesh):
    in_specs = (
        P(("groups", "dom", "sub"), None),
        P(("groups", "dom", "sub"), None),
        P(("groups", "dom", "sub"), None),
        P(("groups", "dom", "sub"), None),
        P(("groups", "dom", "sub"), None),
        P(("groups", "dom", "sub"), None),
        P(None, ("groups", "dom", "sub")),
        P(("groups", "dom", "sub"), None, None),
        P(("groups", "dom", "sub")),
        P(("groups", "dom", "sub")),
        P(("dom", "sub"), None),
        P(("dom", "sub"), None),
        P(("dom", "sub")),
        P(("dom", "sub")),
        P(("dom", "sub")),
        P(("dom", "sub"), None),
        P(("dom", "sub"), None),
        P(("dom", "sub")),
        P(("dom", "sub")),
    )
    out_specs = (
        P(("groups", "dom", "sub"), None),
        P(("groups", "dom", "sub"), None),
        P(("groups", "dom", "sub"), None),
        P(("groups", "dom", "sub"), None),
        P(("groups", "dom", "sub"), None),
        P(("groups", "dom", "sub"), None),
    )
    return jax.shard_map(shards, mesh=mesh, in_specs=in_specs, out_specs=out_specs, check_vma=False)
```

profile of v0, /device:TPU:0, one launch (start us, length us, event | category | flops | bytes accessed | tf_op | source)
XLA Modules:
  0.0 442.2 jit_solution(13776215325105201834)
XLA Ops:
  7.2 0.7 all-gather.7.cloned.1.call-update
  8.0 0.7 all-gather.5.cloned.1.call-update
  8.7 0.7 all-gather.9.cloned.1.call-update
  10.7 1.2 dynamic-slice
  12.6 0.9 dynamic-update-slice
  13.4 0.8 dynamic-update-slice.1
  14.3 0.8 dynamic-update-slice.2
  15.1 0.8 dynamic-update-slice.3
  16.0 0.8 dynamic-update-slice.4
  16.8 63.6 %all-reduce.5 = (f32[512]{0:T(512)S(1)}, f32[512]{0:T(512)S(1)}, f32[512]{0:T(512)S(1)}, f32[512]{0:T(512)S(1)}, f32[512]{0:T(512)S(1)}) all-reduce(f32[512]{0:T(512)S(1)} %dynamic-update-slice.1, f32[512]{0:T(512)S(1)} %dynamic-update-slice.2, f32[512]{0:T(512)S(1)} %dynamic-update-slice.3, ...), channel_id=1, replica_groups=mesh['groups'=2,'dom'=4,'sub'=4] {'dom','sub'}, use_global_device_ids=true, to_apply=%add.1 | all-reduce | flops 2560 | bytes 20480
  80.4 2.5 fusion.44
  83.5 2.4 convolution_multiply_fusion.2
  86.7 3.5 all-gather.5.cloned.1.call-done
  90.2 2.0 fusion.43
  92.5 2.2 scatter_custom_fusion.2
  94.7 2.5 convolution_select_fusion
  97.3 3.2 convolution_multiply_fusion.1
  100.9 0.7 gather_fusion.1
  101.6 31.2 %all-gather.9.cloned.1.call-done = f32[1024,512]{1,0:T(8,128)} async-done(((f32[64,512]{1,0:T(8,128)}), f32[1024,512]{1,0:T(8,128)}) %all-gather.9.cloned.1.call-update) | async-done | bytes 2097168 | tf_op jit(solution)/shard_map/all_gather | solution.py:97
  132.8 3.5 fusion.45
  136.3 1.0 copy-done.5
  137.4 0.8 gather_fusion
  138.4 2.1 convolution_multiply_fusion.3
  140.6 2.2 collective-permute-start.4
  142.8 1.3 collective-permute-start.5
  144.1 2.4 collective-permute-start.6
  146.6 1.3 collective-permute-start.7
  147.9 0.7 collective-permute-done.6
  148.6 4.4 collective-permute-done.7
  153.0 0.8 gather_fusion.2
  153.8 1.5 gather_fusion.3
  155.2 1.1 broadcast_select_fusion
  156.3 1.2 convolution_select_fusion.1
  157.5 4.4 convolution_multiply_fusion
  162.0 17.1 %all-gather.11.cloned.1.call-done = f32[1536,512]{1,0:T(8,128)} async-done(((f32[96,512]{1,0:T(8,128)}), f32[1536,512]{1,0:T(8,128)}) %all-gather.11.cloned.1.call-update) | async-done | bytes 3145744 | tf_op jit(solution)/shard_map/all_gather | solution.py:103
  179.1 5.2 %fusion.46 = f32[128,1536]{1,0:T(8,128)S(1)} fusion(f32[128,512]{1,0:T(8,128)S(1)} %convolution_select_fusion.1, f32[1536,512]{1,0:T(8,128)} %all-gather.11.cloned.1.call-done), kind=kOutput, calls=%fused_computation.115 | convolution fusion | flops 1207959552 | bytes 4194304 | tf_op jit(solution)/shard_map/dot_general | solution.py:42
  184.3 0.8 fusion.42
  185.1 2.3 scatter_custom_fusion
  187.4 1.3 collective-permute-start
  188.7 3.0 collective-permute-start.1
  191.8 1.3 collective-permute-start.2
  193.1 4.5 %collective-permute-start.3 = (f32[1,16,512]{2,1,0:T(8,128)S(1)}, f32[1,16,512]{2,1,0:T(8,128)S(1)}, u32[]{:S(2)}, u32[]{:S(2)}) collective-permute-start(f32[1,16,512]{2,1,0:T(8,128)S(1)} %get-tuple-element.25), channel_id=1, source_target_pairs={{0,1},{1,2},{2,3},{4,5},{5,6},{6,7},{8,9},{9,10},{10,11},{12,13},{... | collective-permute-start | bytes 98312 | tf_op jit(solution)/shard_map/ppermute | solution.py:18
  197.8 1.4 collective-permute-done.3
  199.2 1.2 scatter_fusion
  200.4 38.9 %reduce-scatter.11.cloned.1.call-done = f32[32,512]{1,0:T(8,128)} async-done(((f32[512,512]{1,0:T(8,128)}), f32[32,512]{1,0:T(8,128)}) %reduce-scatter.11.cloned.1.call-update) | async-done | bytes 65552 | tf_op jit(solution)/shard_map/reduce_scatter | solution.py:132
  239.4 65.3 %reduce-scatter.9.cloned.1.call-done = f32[64,512]{1,0:T(8,128)} async-done(((f32[1024,512]{1,0:T(8,128)}), f32[64,512]{1,0:T(8,128)}) %reduce-scatter.9.cloned.1.call-update) | async-done | bytes 131088 | tf_op jit(solution)/shard_map/reduce_scatter | solution.py:126
  304.7 60.6 %reduce-scatter.7.cloned.1.call-done = f32[32,512]{1,0:T(8,128)} async-done(((f32[512,512]{1,0:T(8,128)}), f32[32,512]{1,0:T(8,128)}) %reduce-scatter.7.cloned.1.call-update) | async-done | bytes 65552 | tf_op jit(solution)/shard_map/reduce_scatter | solution.py:146
  365.3 70.1 %reduce-scatter.5.cloned.1.call-done = f32[96,512]{1,0:T(8,128)} async-done(((f32[1536,512]{1,0:T(8,128)}), f32[96,512]{1,0:T(8,128)}) %reduce-scatter.5.cloned.1.call-update) | async-done | bytes 196624 | tf_op jit(solution)/shard_map/reduce_scatter | solution.py:154
  (84 shorter events, 2.7 us)
Async XLA Ops:
  7.2 76.3 %copy-start.2 = (f32[256,512]{1,0:T(8,128)S(1)}, f32[256,512]{1,0:T(8,128)}, u32[]{:S(2)}) copy-start(f32[256,512]{1,0:T(8,128)} %param.22) | copy-start | bytes 1572868
  7.2 76.0 %copy-start.1 = (f32[256,512]{1,0:T(8,128)S(1)}, f32[256,512]{1,0:T(8,128)}, u32[]{:S(2)}) copy-start(f32[256,512]{1,0:T(8,128)} %param.25) | copy-start | bytes 1572868
  7.2 73.2 %all-gather.7.cloned.1.call-start = ((), (), s32[]{:S(2)}) async-start(), calls=%async_computation.5 | async-start | bytes 1114112 | tf_op jit(solution)/shard_map/all_gather | solution.py:98
  7.9 82.3 %all-gather.5.cloned.1.call-start = ((), (), s32[]{:S(2)}) async-start(), calls=%async_computation.4 | async-start | bytes 1114112 | tf_op jit(solution)/shard_map/all_gather | solution.py:104
  8.7 124.1 %all-gather.9.cloned.1.call-start = ((), (), s32[]{:S(2)}) async-start(), calls=%async_computation.6 | async-start | bytes 2228224 | tf_op jit(solution)/shard_map/all_gather | solution.py:97
  9.4 169.7 %all-gather.11.cloned.1.call-start = ((), (), s32[]{:S(2)}) async-start(), calls=%async_computation.7 | async-start | bytes 3342336 | tf_op jit(solution)/shard_map/all_gather | solution.py:103
  10.0 229.4 %reduce-scatter.11.cloned.1.call-start = ((), (), s32[]{:S(2)}) async-start(), calls=%async_computation.11 | async-start | bytes 1114112 | tf_op jit(solution)/shard_map/reduce_scatter | solution.py:132
  82.9 3.0 copy-start.13
  83.0 7.3 %copy-start.7 = (f32[128,512]{1,0:T(8,128)S(1)}, f32[128,512]{1,0:T(8,128)}, u32[]{:S(2)}) copy-start(f32[128,512]{1,0:T(8,128)} %param.24) | copy-start | bytes 786436
  85.9 11.3 %copy-start = (f32[256,512]{1,0:T(8,128)S(1)}, f32[256,512]{1,0:T(8,128)}, u32[]{:S(2)}) copy-start(f32[256,512]{1,0:T(8,128)} %param.21) | copy-start | bytes 1572868
  85.9 218.7 %reduce-scatter.9.cloned.1.call-start = ((), (), s32[]{:S(2)}) async-start(), calls=%async_computation.10 | async-start | bytes 2228224 | tf_op jit(solution)/shard_map/reduce_scatter | solution.py:126
  94.7 2.5 copy-start.8
  97.2 3.5 copy-start.12
  100.5 264.8 %reduce-scatter.7.cloned.1.call-start = ((), (), s32[]{:S(2)}) async-start(), calls=%async_computation.9 | async-start | bytes 1114112 | tf_op jit(solution)/shard_map/reduce_scatter | solution.py:146
  101.6 36.5 %copy-start.9 = (f32[128,512]{1,0:T(8,128)S(1)}, f32[128,512]{1,0:T(8,128)}, u32[]{:S(2)}) copy-start(f32[128,512]{1,0:T(8,128)} %param.26) | copy-start | bytes 786436
  136.3 1.0 copy-start.5
  140.5 294.9 %reduce-scatter.5.cloned.1.call-start = ((), (), s32[]{:S(2)}) async-start(), calls=%async_computation.8 | async-start | bytes 3342336 | tf_op jit(solution)/shard_map/reduce_scatter | solution.py:154
  140.6 7.2 %collective-permute-start.4 = (f32[1,16,512]{2,1,0:T(8,128)S(1)}, f32[1,16,512]{2,1,0:T(8,128)S(1)}, u32[]{:S(2)}, u32[]{:S(2)}) collective-permute-start(f32[1,16,512]{2,1,0:T(8,128)S(1)} %get-tuple-element.28), channel_id=1, source_target_pairs={{0,4},{4,8},{8,12},{1,5},{5,9},{9,13},{2,6},{6,10},{10,14},{3,7},{... | collective-permute-start | bytes 98312 | tf_op jit(solution)/shard_map/ppermute | solution.py:18
  142.8 5.1 %collective-permute-start.5 = (f32[1,16,512]{2,1,0:T(8,128)S(1)}, f32[1,16,512]{2,1,0:T(8,128)S(1)}, u32[]{:S(2)}, u32[]{:S(2)}) collective-permute-start(f32[1,16,512]{2,1,0:T(8,128)S(1)} %get-tuple-element.31), channel_id=1, source_target_pairs={{4,0},{8,4},{12,8},{5,1},{9,5},{13,9},{6,2},{10,6},{14,10},{7,3},{... | collective-permute-start | bytes 98312 | tf_op jit(solution)/shard_map/ppermute | solution.py:20
  144.1 4.4 %collective-permute-start.6 = (f32[1,16,512]{2,1,0:T(8,128)S(1)}, f32[1,16,512]{2,1,0:T(8,128)S(1)}, u32[]{:S(2)}, u32[]{:S(2)}) collective-permute-start(f32[1,16,512]{2,1,0:T(8,128)S(1)} %get-tuple-element.30), channel_id=1, source_target_pairs={{0,1},{1,2},{2,3},{4,5},{5,6},{6,7},{8,9},{9,10},{10,11},{12,13},{... | collective-permute-start | bytes 98312 | tf_op jit(solution)/shard_map/ppermute | solution.py:18
  146.6 6.4 %collective-permute-start.7 = (f32[1,16,512]{2,1,0:T(8,128)S(1)}, f32[1,16,512]{2,1,0:T(8,128)S(1)}, u32[]{:S(2)}, u32[]{:S(2)}) collective-permute-start(f32[1,16,512]{2,1,0:T(8,128)S(1)} %get-tuple-element.29), channel_id=1, source_target_pairs={{1,0},{2,1},{3,2},{5,4},{6,5},{7,6},{9,8},{10,9},{11,10},{13,12},{... | collective-permute-start | bytes 98312 | tf_op jit(solution)/shard_map/ppermute | solution.py:20
  153.0 3.3 copy-start.4
  155.2 2.3 copy-start.11
  161.9 22.4 %copy-start.10 = (f32[128,512]{1,0:T(8,128)S(1)}, f32[128,512]{1,0:T(8,128)}, u32[]{:S(2)}) copy-start(f32[128,512]{1,0:T(8,128)} %param.26) | copy-start | bytes 786436
  162.0 35.7 %copy-start.6 = (f32[256,1024]{1,0:T(8,128)S(1)}, f32[256,1024]{1,0:T(8,128)}, u32[]{:S(2)}) copy-start(f32[256,1024]{1,0:T(8,128)} %copy-done.5) | copy-start | bytes 3145732
  187.4 10.3 %collective-permute-start = (f32[1,16,512]{2,1,0:T(8,128)S(1)}, f32[1,16,512]{2,1,0:T(8,128)S(1)}, u32[]{:S(2)}, u32[]{:S(2)}) collective-permute-start(f32[1,16,512]{2,1,0:T(8,128)S(1)} %get-tuple-element.24), channel_id=1, source_target_pairs={{4,0},{8,4},{12,8},{5,1},{9,5},{13,9},{6,2},{10,6},{14,10},{7,3},{... | collective-permute-start | bytes 98312 | tf_op jit(solution)/shard_map/ppermute | solution.py:20
  188.7 9.1 %collective-permute-start.1 = (f32[1,16,512]{2,1,0:T(8,128)S(1)}, f32[1,16,512]{2,1,0:T(8,128)S(1)}, u32[]{:S(2)}, u32[]{:S(2)}) collective-permute-start(f32[1,16,512]{2,1,0:T(8,128)S(1)} %get-tuple-element.27), channel_id=1, source_target_pairs={{0,4},{4,8},{8,12},{1,5},{5,9},{9,13},{2,6},{6,10},{10,14},{3,7},{... | collective-permute-start | bytes 98312 | tf_op jit(solution)/shard_map/ppermute | solution.py:18
  191.8 6.0 %collective-permute-start.2 = (f32[1,16,512]{2,1,0:T(8,128)S(1)}, f32[1,16,512]{2,1,0:T(8,128)S(1)}, u32[]{:S(2)}, u32[]{:S(2)}) collective-permute-start(f32[1,16,512]{2,1,0:T(8,128)S(1)} %get-tuple-element.26), channel_id=1, source_target_pairs={{1,0},{2,1},{3,2},{5,4},{6,5},{7,6},{9,8},{10,9},{11,10},{13,12},{... | collective-permute-start | bytes 98312 | tf_op jit(solution)/shard_map/ppermute | solution.py:20
  193.1 6.1 %collective-permute-start.3 = (f32[1,16,512]{2,1,0:T(8,128)S(1)}, f32[1,16,512]{2,1,0:T(8,128)S(1)}, u32[]{:S(2)}, u32[]{:S(2)}) collective-permute-start(f32[1,16,512]{2,1,0:T(8,128)S(1)} %get-tuple-element.25), channel_id=1, source_target_pairs={{0,1},{1,2},{2,3},{4,5},{5,6},{6,7},{8,9},{9,10},{10,11},{12,13},{... | collective-permute-start | bytes 98312 | tf_op jit(solution)/shard_map/ppermute | solution.py:18
  200.4 235.0 %copy-start.3 = (f32[256,512]{1,0:T(8,128)}, f32[256,512]{1,0:T(8,128)S(1)}, u32[]{:S(2)}) copy-start(f32[256,512]{1,0:T(8,128)S(1)} %scatter_fusion) | copy-start | bytes 1572868
Sparse Core Ops, SparseCore 0:
  10.2 40.7 all-gather.6
  53.2 36.9 all-gather.4
  92.4 40.3 all-gather.8
  135.0 44.1 all-gather.10
  183.2 56.1 reduce-scatter.10
  244.0 60.6 reduce-scatter.8
  308.9 56.3 reduce-scatter.6
  370.2 65.1 reduce-scatter.4
where the time goes:
time: 443 us; the launch traced here: 442 us
  waiting for transfers between devices  296 us (67%)
  blocking collectives  63.6 us (14%)
  matrix products  29 us (7%)
  starting transfers between devices  17.8 us (4%)
  between operations  16.6 us (4%)
  local copies, waits for them, and re-layouts  10.4 us (2%)
  other arithmetic  8.89 us (2%)
    reduce_scatter x1, waiting for transfers between devices, shards(): lax.psum_scatter(inner(features, edge_grad_pre) * edge_scale, ('dom', 'su...  70.1 us
    reduce_scatter x1, waiting for transfers between devices, shards(): lax.psum_scatter(inner(node_input, node_grad_pre) * node_scale, ('dom', '...  65.3 us
    unnamed x1, blocking collectives  63.6 us
    reduce_scatter x1, waiting for transfers between devices, shards(): lax.psum_scatter(inner(edge_act, edge_grad_z) * edge_scale, ('dom', 'sub'...  60.6 us
    reduce_scatter x1, waiting for transfers between devices, shards(): lax.psum_scatter(inner(node_act, node_grad_z) * node_scale, ('dom', 'sub'...  38.9 us
    all_gather x1, waiting for transfers between devices, shards(): lax.all_gather(node_first, ('dom', 'sub'), axis=0, tiled=True)  31.2 us
    all_gather x1, waiting for transfers between devices, shards(): lax.all_gather(edge_first, ('dom', 'sub'), axis=0, tiled=True)  17.1 us
    dot_general x4, matrix products, outer_back(): lax.dot_general(left, right, (((1,), (1,)), ((), ())), precision=lax.Prec...  12.4 us
  transfers between devices with their start and end apart: 16, of which 10 were waited for; matrix products, arithmetic and copies ran while one was open for 11% of the time, Pallas kernels for 0%

commit v1 on v0

--- a/solution.py
+++ b/solution.py
@@ -5,6 +5,19 @@
 from jax.sharding import PartitionSpec as P
 
 EPSILON = 1e-05
+
+
+def ring_gather(array, axis, dim):
+    count, here, rows = (lax.axis_size(axis), lax.axis_index(axis), array.shape[dim])
+    ahead = [(i, (i + 1) % count) for i in range(count)]
+    out = jnp.zeros((*array.shape[:dim], count * rows, *array.shape[dim + 1 :]), array.dtype)
+    current = array
+    for step in range(count):
+        owner = (here - step) % count
+        out = lax.dynamic_update_slice_in_dim(out, current, owner * rows, axis=dim)
+        if step < count - 1:
+            current = lax.ppermute(current, axis, ahead)
+    return out
 
 
 def padded(cells, sides, width):
@@ -94,7 +107,7 @@
     ghosts = jnp.stack([dom_side[0], dom_side[3], sub_side[0], sub_side[3]])
     ghosts = ghosts.reshape(4 * ghost, width)
     full_node_first, full_node_second, full_node_bias, full_node_gain = (
-        lax.all_gather(node_first, ("dom", "sub"), axis=0, tiled=True),
+        ring_gather(node_first, ("dom", "sub"), 0),
         lax.all_gather(node_second, ("dom", "sub"), axis=0, tiled=True),
         lax.all_gather(node_bias, ("dom", "sub"), axis=0, tiled=True),
         lax.all_gather(node_gain, ("dom", "sub"), axis=0, tiled=True),

time: 443 us -> 458 us (1.034)
  waiting for transfers between devices: 296 us -> 309 us
    ppermute x0 -> x15, waiting for transfers between devices: none -> 102 us  [ring_gather(): current = lax.ppermute(current, axis, ahead)]
    reduce_scatter x1, waiting for transfers between devices: 60.6 us -> 3.72 us  [shards(): lax.psum_scatter(inner(edge_act, edge_grad_z) * edge_scale, ('dom', 'sub'...]
    all_gather x1 -> x0, waiting for transfers between devices: 31.2 us -> none  [shards(): lax.all_gather(node_first, ('dom', 'sub'), axis=0, tiled=True)]
    reduce_scatter x1, waiting for transfers between devices: 38.9 us -> 61 us  [shards(): lax.psum_scatter(inner(node_act, node_grad_z) * node_scale, ('dom', 'sub'...]
    all_gather x1, waiting for transfers between devices: 17.1 us -> 0.01 us  [shards(): lax.all_gather(edge_first, ('dom', 'sub'), axis=0, tiled=True)]
  transfers between devices with their start and end apart: 16 -> 30, of which waited for: 10 -> 21; matrix products, arithmetic and copies ran while one was open for 11% -> 10% of each run, Pallas kernels for 0% -> 0%
where the time goes in v1:
time: 458 us; the launch traced here: 457 us
  waiting for transfers between devices  309 us (67%)
  blocking collectives  63.1 us (14%)
  matrix products  28 us (6%)
  starting transfers between devices  19 us (4%)
  between operations  16.9 us (4%)
  local copies, waits for them, and re-layouts  11.5 us (3%)
  other arithmetic  9.88 us (2%)
    ppermute x15, waiting for transfers between devices, ring_gather(): current = lax.ppermute(current, axis, ahead)  102 us
    reduce_scatter x1, waiting for transfers between devices, shards(): lax.psum_scatter(inner(features, edge_grad_pre) * edge_scale, ('dom', 'su...  70.1 us
    reduce_scatter x1, waiting for transfers between devices, shards(): lax.psum_scatter(inner(node_input, node_grad_pre) * node_scale, ('dom', '...  64.8 us
    unnamed x1, blocking collectives  63.1 us
    reduce_scatter x1, waiting for transfers between devices, shards(): lax.psum_scatter(inner(node_act, node_grad_z) * node_scale, ('dom', 'sub'...  61 us
    dot_general x4, matrix products, inner(): lax.dot_general(left, right, (((0,), (0,)), ((), ())), precision=lax.Prec...  12.1 us
    dot_general x4, matrix products, outer_back(): lax.dot_general(left, right, (((1,), (1,)), ((), ())), precision=lax.Prec...  11.3 us
    ppermute x4, starting transfers between devices, padded(): lax.ppermute(tail, axis, [(i, (i + 1) % count) for i in range(ends)])  10.2 us
  transfers between devices with their start and end apart: 30, of which 21 were waited for; matrix products, arithmetic and copies ran while one was open for 10% of the time, Pallas kernels for 0%

profile of v1, /device:TPU:0, one launch (start us, length us, event | category | flops | bytes accessed | tf_op | source)
XLA Modules:
  0.0 457.3 jit_solution(10529985435853808612)
XLA Ops:
  8.7 3.1 collective-permute-start
  11.8 5.8 %collective-permute-done = f32[64,512]{1,0:T(8,128)S(1)} collective-permute-done((f32[64,512]{1,0:T(8,128)}, f32[64,512]{1,0:T(8,128)S(1)}, u32[]{:S(2)}, u32[]{:S(2)}) %collective-permute-start) | collective-permute-done | bytes 131104 | tf_op jit(solution)/shard_map/ppermute | solution.py:19
  17.6 8.4 %collective-permute-done.1 = f32[64,512]{1,0:T(8,128)S(1)} collective-permute-done((f32[64,512]{1,0:T(8,128)S(1)}, f32[64,512]{1,0:T(8,128)S(1)}, u32[]{:S(2)}, u32[]{:S(2)}) %collective-permute-start.1) | collective-permute-done | bytes 131104 | tf_op jit(solution)/shard_map/ppermute | solution.py:19
  26.0 8.6 %collective-permute-done.2 = f32[64,512]{1,0:T(8,128)S(1)} collective-permute-done((f32[64,512]{1,0:T(8,128)S(1)}, f32[64,512]{1,0:T(8,128)S(1)}, u32[]{:S(2)}, u32[]{:S(2)}) %collective-permute-start.2) | collective-permute-done | bytes 131104 | tf_op jit(solution)/shard_map/ppermute | solution.py:19
  34.7 7.4 %collective-permute-done.3 = f32[64,512]{1,0:T(8,128)S(1)} collective-permute-done((f32[64,512]{1,0:T(8,128)S(1)}, f32[64,512]{1,0:T(8,128)S(1)}, u32[]{:S(2)}, u32[]{:S(2)}) %collective-permute-start.3) | collective-permute-done | bytes 131104 | tf_op jit(solution)/shard_map/ppermute | solution.py:19
  42.2 1.3 compare_and_fusion.1
  43.5 7.4 %collective-permute-done.4 = f32[64,512]{1,0:T(8,128)S(1)} collective-permute-done((f32[64,512]{1,0:T(8,128)S(1)}, f32[64,512]{1,0:T(8,128)S(1)}, u32[]{:S(2)}, u32[]{:S(2)}) %collective-permute-start.4) | collective-permute-done | bytes 131104 | tf_op jit(solution)/shard_map/ppermute | solution.py:19
  52.9 5.1 %collective-permute-done.5 = f32[64,512]{1,0:T(8,128)S(1)} collective-permute-done((f32[64,512]{1,0:T(8,128)S(1)}, f32[64,512]{1,0:T(8,128)S(1)}, u32[]{:S(2)}, u32[]{:S(2)}) %collective-permute-start.5) | collective-permute-done | bytes 131104 | tf_op jit(solution)/shard_map/ppermute | solution.py:19
  58.0 7.1 %collective-permute-done.6 = f32[64,512]{1,0:T(8,128)S(1)} collective-permute-done((f32[64,512]{1,0:T(8,128)S(1)}, f32[64,512]{1,0:T(8,128)S(1)}, u32[]{:S(2)}, u32[]{:S(2)}) %collective-permute-start.6) | collective-permute-done | bytes 131104 | tf_op jit(solution)/shard_map/ppermute | solution.py:19
  65.2 1.2 dynamic-slice
  67.1 0.9 dynamic-update-slice
  69.6 0.8 dynamic-update-slice.3
  71.3 63.1 %all-reduce.5 = (f32[512]{0:T(512)S(1)}, f32[512]{0:T(512)S(1)}, f32[512]{0:T(512)S(1)}, f32[512]{0:T(512)S(1)}, f32[512]{0:T(512)S(1)}) all-reduce(f32[512]{0:T(512)S(1)} %dynamic-update-slice.1, f32[512]{0:T(512)S(1)} %dynamic-update-slice.2, f32[512]{0:T(512)S(1)} %dynamic-update-slice.3, ...), channel_id=1, replica_groups=mesh['groups'=2,'dom'=4,'sub'=4] {'dom','sub'}, use_global_device_ids=true, to_apply=%add.1 | all-reduce | flops 2560 | bytes 20480
  134.8 7.0 %collective-permute-done.8 = f32[64,512]{1,0:T(8,128)S(1)} collective-permute-done((f32[64,512]{1,0:T(8,128)S(1)}, f32[64,512]{1,0:T(8,128)S(1)}, u32[]{:S(2)}, u32[]{:S(2)}) %collective-permute-start.8) | collective-permute-done | bytes 131104 | tf_op jit(solution)/shard_map/ppermute | solution.py:19
  141.9 7.0 %collective-permute-done.9 = f32[64,512]{1,0:T(8,128)S(1)} collective-permute-done((f32[64,512]{1,0:T(8,128)S(1)}, f32[64,512]{1,0:T(8,128)S(1)}, u32[]{:S(2)}, u32[]{:S(2)}) %collective-permute-start.9) | collective-permute-done | bytes 131104 | tf_op jit(solution)/shard_map/ppermute | solution.py:19
  149.0 7.0 %collective-permute-done.10 = f32[64,512]{1,0:T(8,128)S(1)} collective-permute-done((f32[64,512]{1,0:T(8,128)S(1)}, f32[64,512]{1,0:T(8,128)S(1)}, u32[]{:S(2)}, u32[]{:S(2)}) %collective-permute-start.10) | collective-permute-done | bytes 131104 | tf_op jit(solution)/shard_map/ppermute | solution.py:19
  156.1 7.7 %collective-permute-done.11 = f32[64,512]{1,0:T(8,128)S(1)} collective-permute-done((f32[64,512]{1,0:T(8,128)S(1)}, f32[64,512]{1,0:T(8,128)S(1)}, u32[]{:S(2)}, u32[]{:S(2)}) %collective-permute-start.11) | collective-permute-done | bytes 131104 | tf_op jit(solution)/shard_map/ppermute | solution.py:19
  163.9 8.3 %collective-permute-done.12 = f32[64,512]{1,0:T(8,128)S(1)} collective-permute-done((f32[64,512]{1,0:T(8,128)S(1)}, f32[64,512]{1,0:T(8,128)S(1)}, u32[]{:S(2)}, u32[]{:S(2)}) %collective-permute-start.12) | collective-permute-done | bytes 131104 | tf_op jit(solution)/shard_map/ppermute | solution.py:19
  172.2 7.4 %collective-permute-done.13 = f32[64,512]{1,0:T(8,128)S(1)} collective-permute-done((f32[64,512]{1,0:T(8,128)S(1)}, f32[64,512]{1,0:T(8,128)S(1)}, u32[]{:S(2)}, u32[]{:S(2)}) %collective-permute-start.13) | collective-permute-done | bytes 131104 | tf_op jit(solution)/shard_map/ppermute | solution.py:19
  179.6 7.0 %collective-permute-done.14 = f32[64,512]{1,0:T(8,128)S(1)} collective-permute-done((f32[64,512]{1,0:T(8,128)S(1)}, f32[64,512]{1,0:T(8,128)S(1)}, u32[]{:S(2)}, u32[]{:S(2)}) %collective-permute-start.14) | collective-permute-done | bytes 131104 | tf_op jit(solution)/shard_map/ppermute | solution.py:19
  186.7 2.6 fusion.44
  189.9 2.3 convolution_select_fusion
  192.1 1.9 fusion.45
  194.1 1.0 copy-done.7
  196.1 2.0 fusion.43
  198.6 2.1 convolution_multiply_fusion.3
  201.0 2.3 convolution_multiply_fusion.2
  204.0 1.6 scatter_custom_fusion.2
  205.6 3.2 convolution_multiply_fusion.1
  209.9 1.3 collective-permute-start.19
  211.2 1.3 collective-permute-start.20
  212.5 1.3 collective-permute-start.21
  213.8 1.3 collective-permute-start.22
  215.3 4.4 collective-permute-done.22
  222.2 1.9 convolution_select_fusion.1
  224.1 4.4 convolution_multiply_fusion
  229.2 5.3 %fusion.46 = f32[128,1536]{1,0:T(8,128)S(1)} fusion(f32[128,512]{1,0:T(8,128)S(1)} %convolution_select_fusion.1, f32[1536,512]{1,0:T(8,128)} %all-gather.8.cloned.1.call-done), kind=kOutput, calls=%fused_computation.131 | convolution fusion | flops 1207959552 | bytes 4194304 | tf_op jit(solution)/shard_map/dot_general | solution.py:55
  235.3 2.3 scatter_custom_fusion
  237.6 1.3 collective-permute-start.15
  238.9 3.0 collective-permute-start.16
  241.9 1.3 collective-permute-start.17
  243.2 4.5 collective-permute-start.18
  247.9 1.7 collective-permute-done.18
  249.6 1.2 scatter_fusion
  250.8 3.7 reduce-scatter.7.cloned.1.call-done
  254.6 61.0 %reduce-scatter.11.cloned.1.call-done = f32[32,512]{1,0:T(8,128)} async-done(((f32[512,512]{1,0:T(8,128)}), f32[32,512]{1,0:T(8,128)}) %reduce-scatter.11.cloned.1.call-update) | async-done | bytes 65552 | tf_op jit(solution)/shard_map/reduce_scatter | solution.py:145
  315.5 64.8 %reduce-scatter.9.cloned.1.call-done = f32[64,512]{1,0:T(8,128)} async-done(((f32[1024,512]{1,0:T(8,128)}), f32[64,512]{1,0:T(8,128)}) %reduce-scatter.9.cloned.1.call-update) | async-done | bytes 131088 | tf_op jit(solution)/shard_map/reduce_scatter | solution.py:139
  380.4 70.1 %reduce-scatter.5.cloned.1.call-done = f32[96,512]{1,0:T(8,128)} async-done(((f32[1536,512]{1,0:T(8,128)}), f32[96,512]{1,0:T(8,128)}) %reduce-scatter.5.cloned.1.call-update) | async-done | bytes 196624 | tf_op jit(solution)/shard_map/reduce_scatter | solution.py:167
  (152 shorter events, 13.4 us)
Async XLA Ops:
  7.2 127.5 %copy-start.15 = (f32[64,512]{1,0:T(8,128)S(1)}, f32[64,512]{1,0:T(8,128)}, u32[]{:S(2)}) copy-start(f32[64,512]{1,0:T(8,128)} %param.36) | copy-start | bytes 393220
  7.2 179.5 %all-gather.6.cloned.1.call-start = ((), (), s32[]{:S(2)}) async-start(), calls=%async_computation.5 | async-start | bytes 1114112 | tf_op jit(solution)/shard_map/all_gather | solution.py:111
  7.9 188.0 %all-gather.4.cloned.1.call-start = ((), (), s32[]{:S(2)}) async-start(), calls=%async_computation.4 | async-start | bytes 1114112 | tf_op jit(solution)/shard_map/all_gather | solution.py:117
  8.7 220.5 %all-gather.8.cloned.1.call-start = ((), (), s32[]{:S(2)}) async-start(), calls=%async_computation.6 | async-start | bytes 3342336 | tf_op jit(solution)/shard_map/all_gather | solution.py:116
  8.7 8.9 %collective-permute-start = (f32[64,512]{1,0:T(8,128)}, f32[64,512]{1,0:T(8,128)S(1)}, u32[]{:S(2)}, u32[]{:S(2)}) collective-permute-start(f32[64,512]{1,0:T(8,128)} %param.36), channel_id=1, source_target_pairs={{0,1},{1,2},{2,3},{3,4},{4,5},{5,6},{6,7},{7,8},{8,9},{9,10},{10,1... | collective-permute-start | bytes 393224 | tf_op jit(solution)/shard_map/ppermute | solution.py:19
  17.6 8.4 %collective-permute-start.1 = (f32[64,512]{1,0:T(8,128)S(1)}, f32[64,512]{1,0:T(8,128)S(1)}, u32[]{:S(2)}, u32[]{:S(2)}) collective-permute-start(f32[64,512]{1,0:T(8,128)S(1)} %collective-permute-done), channel_id=1, source_target_pairs={{0,1},{1,2},{2,3},{3,4},{4,5},{5,6},{6,7},{7,8},{8,9},{9,10},{10,1... | collective-permute-start | bytes 393224 | tf_op jit(solution)/shard_map/ppermute | solution.py:19
  26.0 8.6 %collective-permute-start.2 = (f32[64,512]{1,0:T(8,128)S(1)}, f32[64,512]{1,0:T(8,128)S(1)}, u32[]{:S(2)}, u32[]{:S(2)}) collective-permute-start(f32[64,512]{1,0:T(8,128)S(1)} %collective-permute-done.1), channel_id=1, source_target_pairs={{0,1},{1,2},{2,3},{3,4},{4,5},{5,6},{6,7},{7,8},{8,9},{9,10},{10,1... | collective-permute-start | bytes 393224 | tf_op jit(solution)/shard_map/ppermute | solution.py:19
  34.7 7.5 %collective-permute-start.3 = (f32[64,512]{1,0:T(8,128)S(1)}, f32[64,512]{1,0:T(8,128)S(1)}, u32[]{:S(2)}, u32[]{:S(2)}) collective-permute-start(f32[64,512]{1,0:T(8,128)S(1)} %collective-permute-done.2), channel_id=1, source_target_pairs={{0,1},{1,2},{2,3},{3,4},{4,5},{5,6},{6,7},{7,8},{8,9},{9,10},{10,1... | collective-permute-start | bytes 393224 | tf_op jit(solution)/shard_map/ppermute | solution.py:19
  34.7 219.9 %reduce-scatter.7.cloned.1.call-start = ((), (), s32[]{:S(2)}) async-start(), calls=%async_computation.8 | async-start | bytes 1114112 | tf_op jit(solution)/shard_map/reduce_scatter | solution.py:159
  42.2 8.7 %collective-permute-start.4 = (f32[64,512]{1,0:T(8,128)S(1)}, f32[64,512]{1,0:T(8,128)S(1)}, u32[]{:S(2)}, u32[]{:S(2)}) collective-permute-start(f32[64,512]{1,0:T(8,128)S(1)} %collective-permute-done.3), channel_id=1, source_target_pairs={{0,1},{1,2},{2,3},{3,4},{4,5},{5,6},{6,7},{7,8},{8,9},{9,10},{10,1... | collective-permute-start | bytes 393224 | tf_op jit(solution)/shard_map/ppermute | solution.py:19
  50.9 7.1 %collective-permute-start.5 = (f32[64,512]{1,0:T(8,128)S(1)}, f32[64,512]{1,0:T(8,128)S(1)}, u32[]{:S(2)}, u32[]{:S(2)}) collective-permute-start(f32[64,512]{1,0:T(8,128)S(1)} %collective-permute-done.4), channel_id=1, source_target_pairs={{0,1},{1,2},{2,3},{3,4},{4,5},{5,6},{6,7},{7,8},{8,9},{9,10},{10,1... | collective-permute-start | bytes 393224 | tf_op jit(solution)/shard_map/ppermute | solution.py:19
  58.0 7.2 %collective-permute-start.6 = (f32[64,512]{1,0:T(8,128)S(1)}, f32[64,512]{1,0:T(8,128)S(1)}, u32[]{:S(2)}, u32[]{:S(2)}) collective-permute-start(f32[64,512]{1,0:T(8,128)S(1)} %collective-permute-done.5), channel_id=1, source_target_pairs={{0,1},{1,2},{2,3},{3,4},{4,5},{5,6},{6,7},{7,8},{8,9},{9,10},{10,1... | collective-permute-start | bytes 393224 | tf_op jit(solution)/shard_map/ppermute | solution.py:19
  58.0 146.0 %copy-start.17 = (f32[128]{0:T(128)}, f32[128]{0:T(128)S(1)}, u32[]{:S(2)}) copy-start(f32[128]{0:T(128)S(1)} %compare_convert_fusion) | copy-start | bytes 1540
  65.2 69.5 %collective-permute-start.7 = (f32[64,512]{1,0:T(8,128)S(1)}, f32[64,512]{1,0:T(8,128)S(1)}, u32[]{:S(2)}, u32[]{:S(2)}) collective-permute-start(f32[64,512]{1,0:T(8,128)S(1)} %collective-permute-done.6), channel_id=1, source_target_pairs={{0,1},{1,2},{2,3},{3,4},{4,5},{5,6},{6,7},{7,8},{8,9},{9,10},{10,1... | collective-permute-start | bytes 393224 | tf_op jit(solution)/shard_map/ppermute | solution.py:19
  134.7 7.1 %collective-permute-start.8 = (f32[64,512]{1,0:T(8,128)S(1)}, f32[64,512]{1,0:T(8,128)S(1)}, u32[]{:S(2)}, u32[]{:S(2)}) collective-permute-start(f32[64,512]{1,0:T(8,128)S(1)} %collective-permute-done.7), channel_id=1, source_target_pairs={{0,1},{1,2},{2,3},{3,4},{4,5},{5,6},{6,7},{7,8},{8,9},{9,10},{10,1... | collective-permute-start | bytes 393224 | tf_op jit(solution)/shard_map/ppermute | solution.py:19
  141.9 7.1 %collective-permute-start.9 = (f32[64,512]{1,0:T(8,128)S(1)}, f32[64,512]{1,0:T(8,128)S(1)}, u32[]{:S(2)}, u32[]{:S(2)}) collective-permute-start(f32[64,512]{1,0:T(8,128)S(1)} %collective-permute-done.8), channel_id=1, source_target_pairs={{0,1},{1,2},{2,3},{3,4},{4,5},{5,6},{6,7},{7,8},{8,9},{9,10},{10,1... | collective-permute-start | bytes 393224 | tf_op jit(solution)/shard_map/ppermute | solution.py:19
  149.0 7.1 %collective-permute-start.10 = (f32[64,512]{1,0:T(8,128)S(1)}, f32[64,512]{1,0:T(8,128)S(1)}, u32[]{:S(2)}, u32[]{:S(2)}) collective-permute-start(f32[64,512]{1,0:T(8,128)S(1)} %collective-permute-done.9), channel_id=1, source_target_pairs={{0,1},{1,2},{2,3},{3,4},{4,5},{5,6},{6,7},{7,8},{8,9},{9,10},{10,1... | collective-permute-start | bytes 393224 | tf_op jit(solution)/shard_map/ppermute | solution.py:19
  156.0 7.8 %collective-permute-start.11 = (f32[64,512]{1,0:T(8,128)S(1)}, f32[64,512]{1,0:T(8,128)S(1)}, u32[]{:S(2)}, u32[]{:S(2)}) collective-permute-start(f32[64,512]{1,0:T(8,128)S(1)} %collective-permute-done.10), channel_id=1, source_target_pairs={{0,1},{1,2},{2,3},{3,4},{4,5},{5,6},{6,7},{7,8},{8,9},{9,10},{10,1... | collective-permute-start | bytes 393224 | tf_op jit(solution)/shard_map/ppermute | solution.py:19
  163.8 8.3 %collective-permute-start.12 = (f32[64,512]{1,0:T(8,128)S(1)}, f32[64,512]{1,0:T(8,128)S(1)}, u32[]{:S(2)}, u32[]{:S(2)}) collective-permute-start(f32[64,512]{1,0:T(8,128)S(1)} %collective-permute-done.11), channel_id=1, source_target_pairs={{0,1},{1,2},{2,3},{3,4},{4,5},{5,6},{6,7},{7,8},{8,9},{9,10},{10,1... | collective-permute-start | bytes 393224 | tf_op jit(solution)/shard_map/ppermute | solution.py:19
  163.8 25.7 %copy-start.1 = (f32[256,512]{1,0:T(8,128)S(1)}, f32[256,512]{1,0:T(8,128)}, u32[]{:S(2)}) copy-start(f32[256,512]{1,0:T(8,128)} %param.25) | copy-start | bytes 1572868
  172.1 7.4 %collective-permute-start.13 = (f32[64,512]{1,0:T(8,128)S(1)}, f32[64,512]{1,0:T(8,128)S(1)}, u32[]{:S(2)}, u32[]{:S(2)}) collective-permute-start(f32[64,512]{1,0:T(8,128)S(1)} %collective-permute-done.12), channel_id=1, source_target_pairs={{0,1},{1,2},{2,3},{3,4},{4,5},{5,6},{6,7},{7,8},{8,9},{9,10},{10,1... | collective-permute-start | bytes 393224 | tf_op jit(solution)/shard_map/ppermute | solution.py:19
  179.6 7.1 %collective-permute-start.14 = (f32[64,512]{1,0:T(8,128)S(1)}, f32[64,512]{1,0:T(8,128)S(1)}, u32[]{:S(2)}, u32[]{:S(2)}) collective-permute-start(f32[64,512]{1,0:T(8,128)S(1)} %collective-permute-done.13), channel_id=1, source_target_pairs={{0,1},{1,2},{2,3},{3,4},{4,5},{5,6},{6,7},{7,8},{8,9},{9,10},{10,1... | collective-permute-start | bytes 393224 | tf_op jit(solution)/shard_map/ppermute | solution.py:19
  186.7 3.2 copy-start.9
  195.2 3.2 copy-start.12
  198.1 2.9 copy-start.4
  198.6 4.8 %copy-start.20 = (f32[128]{0:T(128)}, f32[128]{0:T(128)S(1)}, u32[]{:S(2)}) copy-start(f32[128]{0:T(128)S(1)} %broadcast_multiply_fusion.3) | copy-start | bytes 1540
  200.8 2.6 copy-start.19
  200.8 4.8 %copy-start = (f32[256,512]{1,0:T(8,128)S(1)}, f32[256,512]{1,0:T(8,128)}, u32[]{:S(2)}) copy-start(f32[256,512]{1,0:T(8,128)} %param.21) | copy-start | bytes 1572868
  200.8 4.8 %copy-start.3 = (f32[256,512]{1,0:T(8,128)S(1)}, f32[256,512]{1,0:T(8,128)}, u32[]{:S(2)}) copy-start(f32[256,512]{1,0:T(8,128)} %copy-done.2) | copy-start | bytes 1572868
  200.8 114.7 %reduce-scatter.11.cloned.1.call-start = ((), (), s32[]{:S(2)}) async-start(), calls=%async_computation.10 | async-start | bytes 1114112 | tf_op jit(solution)/shard_map/reduce_scatter | solution.py:145
  203.4 177.0 %reduce-scatter.9.cloned.1.call-start = ((), (), s32[]{:S(2)}) async-start(), calls=%async_computation.9 | async-start | bytes 2228224 | tf_op jit(solution)/shard_map/reduce_scatter | solution.py:139
  205.6 3.3 copy-start.16
  208.8 241.6 %reduce-scatter.5.cloned.1.call-start = ((), (), s32[]{:S(2)}) async-start(), calls=%async_computation.7 | async-start | bytes 3342336 | tf_op jit(solution)/shard_map/reduce_scatter | solution.py:167
  209.0 10.8 %copy-start.22 = (s32[64]{0:T(128)}, s32[64]{0:T(128)S(1)}, u32[]{:S(2)}) copy-start(s32[64]{0:T(128)S(1)} %reshape.204) | copy-start | bytes 772
  209.9 5.2 %collective-permute-start.19 = (f32[1,16,512]{2,1,0:T(8,128)S(1)}, f32[1,16,512]{2,1,0:T(8,128)S(1)}, u32[]{:S(2)}, u32[]{:S(2)}) collective-permute-start(f32[1,16,512]{2,1,0:T(8,128)S(1)} %get-tuple-element.28), channel_id=1, source_target_pairs={{0,4},{4,8},{8,12},{1,5},{5,9},{9,13},{2,6},{6,10},{10,14},{3,7},{... | collective-permute-start | bytes 98312 | tf_op jit(solution)/shard_map/ppermute | solution.py:31
  211.2 3.9 collective-permute-start.20
  212.5 2.9 collective-permute-start.21
  213.8 6.0 %collective-permute-start.22 = (f32[1,16,512]{2,1,0:T(8,128)S(1)}, f32[1,16,512]{2,1,0:T(8,128)S(1)}, u32[]{:S(2)}, u32[]{:S(2)}) collective-permute-start(f32[1,16,512]{2,1,0:T(8,128)S(1)} %get-tuple-element.29), channel_id=1, source_target_pairs={{1,0},{2,1},{3,2},{5,4},{6,5},{7,6},{9,8},{10,9},{11,10},{13,12},{... | collective-permute-start | bytes 98312 | tf_op jit(solution)/shard_map/ppermute | solution.py:33
  221.4 2.7 copy-start.14
  229.1 5.3 %copy-start.13 = (f32[128,512]{1,0:T(8,128)S(1)}, f32[128,512]{1,0:T(8,128)}, u32[]{:S(2)}) copy-start(f32[128,512]{1,0:T(8,128)} %param.26) | copy-start | bytes 786436
  229.2 5.3 %copy-start.18 = (f32[128]{0:T(128)S(1)}, f32[128]{0:T(128)}, u32[]{:S(2)}) copy-start(f32[128]{0:T(128)} %copy-done.17) | copy-start | bytes 1540
  234.5 13.3 %copy-start.8 = (f32[256,1024]{1,0:T(8,128)S(1)}, f32[256,1024]{1,0:T(8,128)}, u32[]{:S(2)}) copy-start(f32[256,1024]{1,0:T(8,128)} %copy-done.7) | copy-start | bytes 3145732
  235.3 14.4 %copy-start.23 = (s32[64]{0:T(128)S(1)}, s32[64]{0:T(128)}, u32[]{:S(2)}) copy-start(s32[64]{0:T(128)} %copy-done.22) | copy-start | bytes 772
  237.6 10.3 %collective-permute-start.15 = (f32[1,16,512]{2,1,0:T(8,128)S(1)}, f32[1,16,512]{2,1,0:T(8,128)S(1)}, u32[]{:S(2)}, u32[]{:S(2)}) collective-permute-start(f32[1,16,512]{2,1,0:T(8,128)S(1)} %get-tuple-element.24), channel_id=1, source_target_pairs={{4,0},{8,4},{12,8},{5,1},{9,5},{13,9},{6,2},{10,6},{14,10},{7,3},{... | collective-permute-start | bytes 98312 | tf_op jit(solution)/shard_map/ppermute | solution.py:33
  238.9 9.1 %collective-permute-start.16 = (f32[1,16,512]{2,1,0:T(8,128)S(1)}, f32[1,16,512]{2,1,0:T(8,128)S(1)}, u32[]{:S(2)}, u32[]{:S(2)}) collective-permute-start(f32[1,16,512]{2,1,0:T(8,128)S(1)} %get-tuple-element.27), channel_id=1, source_target_pairs={{0,4},{4,8},{8,12},{1,5},{5,9},{9,13},{2,6},{6,10},{10,14},{3,7},{... | collective-permute-start | bytes 98312 | tf_op jit(solution)/shard_map/ppermute | solution.py:31
  241.9 6.0 %collective-permute-start.17 = (f32[1,16,512]{2,1,0:T(8,128)S(1)}, f32[1,16,512]{2,1,0:T(8,128)S(1)}, u32[]{:S(2)}, u32[]{:S(2)}) collective-permute-start(f32[1,16,512]{2,1,0:T(8,128)S(1)} %get-tuple-element.26), channel_id=1, source_target_pairs={{1,0},{2,1},{3,2},{5,4},{6,5},{7,6},{9,8},{10,9},{11,10},{13,12},{... | collective-permute-start | bytes 98312 | tf_op jit(solution)/shard_map/ppermute | solution.py:33
  243.2 6.4 %collective-permute-start.18 = (f32[1,16,512]{2,1,0:T(8,128)S(1)}, f32[1,16,512]{2,1,0:T(8,128)S(1)}, u32[]{:S(2)}, u32[]{:S(2)}) collective-permute-start(f32[1,16,512]{2,1,0:T(8,128)S(1)} %get-tuple-element.25), channel_id=1, source_target_pairs={{0,1},{1,2},{2,3},{4,5},{5,6},{6,7},{8,9},{9,10},{10,11},{12,13},{... | collective-permute-start | bytes 98312 | tf_op jit(solution)/shard_map/ppermute | solution.py:31
  250.8 199.6 %copy-start.5 = (f32[256,512]{1,0:T(8,128)}, f32[256,512]{1,0:T(8,128)S(1)}, u32[]{:S(2)}) copy-start(f32[256,512]{1,0:T(8,128)S(1)} %scatter_fusion) | copy-start | bytes 1572868
  (8 other events, 10.5 us)
Sparse Core Ops, SparseCore 0:
  10.2 42.8 all-gather.5
  55.3 36.5 all-gather.3
  94.2 44.7 all-gather.7
  200.9 53.6 reduce-scatter.6
  259.0 56.4 reduce-scatter.10
  319.7 60.6 reduce-scatter.8
  385.2 65.1 reduce-scatter.4
